TPU v7x, 128 devices: a whole 4x4x4 slice. The times are simulated.
128 devices in a mesh: dp: 16 (over x, y), fsdp: 8 (over z, core).
Axes of the slice: x: 4, y: 4, z: 4, core: 2. Of those that a mesh axis runs over, the one named last changes fastest.
Arguments:
- page_embed: bfloat16 [81920, 2048], P(('dp', 'fsdp')), may hold values from -6 to 6
- page_slot: int32 [81920], P(('dp', 'fsdp')), may hold values from 0 to 10239, as said below
- doc_ids: int32 [128, 640], P(('dp', 'fsdp')), may hold values from 0 to 9, never falling along the last dimension, each value on 1 to 128 neighbouring positions
- qkv_weight: bfloat16 [3, 2048, 1024], P(None, 'fsdp'), may hold values from -0.125 to 0.125
- out_weight: bfloat16 [1024, 2048], P(None, 'fsdp'), may hold values from -0.1875 to 0.1875
- fig_slot: int32 [2048], P(('dp', 'fsdp')), may hold values from 0 to 639
- cap_slot: int32 [2048], P(('dp', 'fsdp')), may hold values from 0 to 639
- logit_scale: float32 [1], replicated, may hold values from 10 to 30
- loss_cotangent: float32 [2048], P(('dp', 'fsdp')), may hold values from 8 to 64
Outputs:
- page_grad: bfloat16 [81920, 2048], P(('dp', 'fsdp'))
- pair_loss: float32 [2048], P(('dp', 'fsdp'))
Inputs may be any that keep to these rules, and one draw needn't show every extreme that they name: page_slot // 640 is the dp index of the owner and page_slot % 640 the slot there; within each group every slot is named by exactly one page; one device sends at most 50 pages to one owner, and every device sends exactly 50 to some owners. `doc_ids`: along a device's slots the document number never falls; each of the 10 documents has 1 to 128 slots, one exactly 128. `fig_slot`: a slot of the pair's own device. `cap_slot`: a slot of the pair's own device.
All inputs are finite; a program needn't handle non-finite values.
Results may differ from a plain program's by a relative error of at most 0.017.
Values may be sent and summed in bfloat16 or wider, within the bound.
No kernel may reach another device: no remote copies, remote signals or barrier semaphores. Data moves between devices by JAX's collectives and lax.ppermute only.
A program may use at most 192 MiB of HBM per device.

v0:
```python
import math
import jax
import jax.numpy as jnp
from jax import lax
from jax.sharding import PartitionSpec as P

HD = 64
EPSILON = 1e-06


def log_total(values, axis):
    return jnp.log(jnp.sum(jnp.exp(values), axis=axis))


def attend(query_h, key_value, out_mat, query_doc, doc_row):
    query_count = query_h.shape[0]
    row_count = key_value.shape[0]
    head_width = query_h.shape[1]
    query_h = query_h.reshape(query_count, -1, HD)
    key_h = key_value[:, :head_width].reshape(row_count, -1, HD)
    value_h = key_value[:, head_width:].reshape(row_count, -1, HD)
    scores = jnp.einsum("qhd,khd->hqk", query_h, key_h, preferred_element_type=jnp.float32) * (
        1.0 / math.sqrt(HD)
    )
    same_doc = query_doc[:, None] == doc_row[None, :]
    scores = jnp.where(same_doc[None], scores, -1e30)
    weights = jnp.exp(scores)
    attn_prob = (weights / jnp.sum(weights, axis=2, keepdims=True)).astype(jnp.bfloat16)
    mixed = jnp.einsum("hqk,khd->qhd", attn_prob, value_h, preferred_element_type=jnp.float32)
    mixed = mixed.astype(jnp.bfloat16).reshape(query_count, -1)
    return jnp.dot(mixed, out_mat, preferred_element_type=jnp.float32)


def select_rows(onehot, rows):
    picked = jnp.dot(onehot, rows, preferred_element_type=jnp.float32)
    return picked.astype(rows.dtype)


def select_rows_t(onehot, rows):
    picked = lax.dot_general(
        onehot, rows, (((0,), (0,)), ((), ())), preferred_element_type=jnp.float32
    )
    return picked.astype(rows.dtype)


def body(
    page_embed,
    page_slot,
    doc_ids,
    qkv_weight,
    out_weight,
    fig_slot,
    cap_slot,
    logit_scale,
    loss_cotangent,
):
    dp_count = lax.axis_size("dp")
    row_count = page_embed.shape[0]
    feature_width = page_embed.shape[1]
    capacity = 5 * row_count // (4 * dp_count)
    buffer_rows = dp_count * capacity
    owner_idx = page_slot // row_count
    slot_idx = page_slot % row_count
    onehot = (owner_idx[:, None] == jnp.arange(dp_count)[None, :]).astype(jnp.int32)
    rank_idx = jnp.sum((jnp.cumsum(onehot, axis=0) - onehot) * onehot, axis=1)
    dest = owner_idx * capacity + rank_idx
    send_match = dest[None, :] == jnp.arange(buffer_rows)[:, None]
    send_ids = jnp.where(
        jnp.any(send_match, axis=1),
        jnp.sum(jnp.where(send_match, slot_idx[None, :], 0), axis=1),
        row_count,
    ).reshape(dp_count, capacity)
    send_onehot = jnp.concatenate(
        [
            send_match.astype(jnp.bfloat16).reshape(dp_count, capacity, row_count),
            jnp.zeros((dp_count, 1, row_count), jnp.bfloat16),
        ],
        axis=1,
    )
    id_lanes = jnp.zeros((dp_count, feature_width), jnp.float32)
    id_lanes = id_lanes.at[:, :capacity].set((send_ids // 16).astype(jnp.float32))
    id_lanes = id_lanes.at[:, 128 : 128 + capacity].set((send_ids % 16).astype(jnp.float32))
    id_rows = jnp.concatenate(
        [jnp.zeros((dp_count, capacity, feature_width), jnp.float32), id_lanes[:, None, :]], axis=1
    )
    send_rows = (
        jnp.einsum("opk,kd->opd", send_onehot, page_embed, preferred_element_type=jnp.float32)
        + id_rows
    ).astype(jnp.bfloat16)
    recv_rows = lax.all_to_all(send_rows, "dp", split_axis=0, concat_axis=0, tiled=True)
    id_row = recv_rows[:, capacity, :].astype(jnp.float32)
    recv_ids = id_row[:, :capacity].astype(jnp.int32) * 16 + id_row[:, 128 : 128 + capacity].astype(
        jnp.int32
    )
    recv_ids = jnp.concatenate([recv_ids, jnp.full((dp_count, 1), row_count, jnp.int32)], axis=1)
    recv_onehot = (jnp.arange(row_count)[:, None, None] == recv_ids[None, :, :]).astype(
        jnp.bfloat16
    )
    slot_row_block = jnp.einsum(
        "sop,opd->sd", recv_onehot, recv_rows, preferred_element_type=jnp.float32
    ).astype(jnp.bfloat16)
    qkv_full, out_full = (
        lax.all_gather(qkv_weight, "fsdp", axis=1, tiled=True),
        lax.all_gather(out_weight, "fsdp", axis=1, tiled=True),
    )
    kv_full = jnp.concatenate([qkv_full[1], qkv_full[2]], axis=1)
    doc_row = doc_ids[0]
    pair_count = fig_slot.shape[0]
    query_slots = jnp.concatenate([fig_slot, cap_slot], axis=0)
    query_onehot = (query_slots[:, None] == jnp.arange(row_count)[None, :]).astype(jnp.bfloat16)
    query_doc = jnp.sum(
        jnp.where(query_slots[:, None] == jnp.arange(row_count)[None, :], doc_row[None, :], 0),
        axis=1,
    )
    query_rows = select_rows(query_onehot, slot_row_block)
    query_h = jnp.dot(query_rows, qkv_full[0], preferred_element_type=jnp.float32).astype(
        jnp.bfloat16
    )
    key_value = jnp.dot(slot_row_block, kv_full, preferred_element_type=jnp.float32).astype(
        jnp.bfloat16
    )

    def branch(query_in, key_value_in):
        return attend(query_in, key_value_in, out_full, query_doc, doc_row)

    attn_out, pullback = jax.vjp(branch, query_h, key_value)
    query_output = query_rows.astype(jnp.float32) + attn_out
    fig_vec = query_output[:pair_count]
    cap_vec = query_output[pair_count:]
    fig_inv = lax.rsqrt(jnp.sum(fig_vec * fig_vec, axis=1, keepdims=True) + EPSILON)
    cap_inv = lax.rsqrt(jnp.sum(cap_vec * cap_vec, axis=1, keepdims=True) + EPSILON)
    fig_unit = fig_vec * fig_inv
    cap_unit = cap_vec * cap_inv
    fig_emb = fig_unit.astype(jnp.bfloat16)
    cap_emb = cap_unit.astype(jnp.bfloat16)
    weight_hi = loss_cotangent.astype(jnp.bfloat16)
    weight_lo = (loss_cotangent - weight_hi.astype(jnp.float32)).astype(jnp.bfloat16)
    weight_lanes = jnp.zeros((2 * pair_count, 128), jnp.bfloat16)
    weight_lanes = weight_lanes.at[:pair_count, 0].set(weight_hi).at[:pair_count, 1].set(weight_lo)
    both_emb = jnp.concatenate([jnp.concatenate([fig_emb, cap_emb], axis=0), weight_lanes], axis=1)
    all_both = lax.all_to_all(
        jnp.broadcast_to(both_emb[None], (dp_count,) + both_emb.shape),
        "dp",
        split_axis=0,
        concat_axis=0,
        tiled=True,
    )
    all_fig = all_both[:, :pair_count, :feature_width].reshape(-1, feature_width)
    all_cap = all_both[:, pair_count:, :feature_width].reshape(-1, feature_width)
    all_weight = (
        all_both[:, :pair_count, feature_width].astype(jnp.float32)
        + all_both[:, :pair_count, feature_width + 1].astype(jnp.float32)
    ).reshape(-1)
    logit_mult = logit_scale[0]
    pair_total = all_fig.shape[0]
    first_pair = lax.axis_index("dp") * pair_count
    logits = logit_mult * jnp.dot(all_fig, all_cap.T, preferred_element_type=jnp.float32)
    row_lse = log_total(logits, 1)
    col_lse = log_total(logits, 0)
    eye_mat = jnp.eye(pair_total, dtype=jnp.float32)
    diag_logit = jnp.sum(logits * eye_mat, axis=1)
    own_rows = first_pair + jnp.arange(pair_count)
    own_mask = (jnp.arange(pair_total)[None, :] == own_rows[:, None]).astype(jnp.float32)
    loss_all = 0.5 * (row_lse - diag_logit) + 0.5 * (col_lse - diag_logit)
    pair_loss = jnp.dot(own_mask, loss_all, precision=lax.Precision.HIGHEST)
    prob_rows = jnp.exp(logits - row_lse[:, None])
    prob_cols = jnp.exp(logits - col_lse[None, :])
    coef = (
        0.5 * all_weight[:, None] * (prob_rows - eye_mat)
        + 0.5 * (prob_cols - eye_mat) * all_weight[None, :]
    )
    coef_rows = jnp.dot(own_mask, coef, precision=lax.Precision.HIGHEST)
    coef_cols = jnp.dot(own_mask, coef.T, precision=lax.Precision.HIGHEST)
    fig_grad = logit_mult * jnp.dot(
        coef_rows, all_cap.astype(jnp.float32), precision=lax.Precision.HIGHEST
    )
    cap_grad = logit_mult * jnp.dot(
        coef_cols, all_fig.astype(jnp.float32), precision=lax.Precision.HIGHEST
    )
    figure_direction = fig_inv * (
        fig_grad - fig_unit * jnp.sum(fig_unit * fig_grad, axis=1, keepdims=True)
    )
    caption_direction = cap_inv * (
        cap_grad - cap_unit * jnp.sum(cap_unit * cap_grad, axis=1, keepdims=True)
    )
    query_ct = jnp.concatenate([figure_direction, caption_direction], axis=0)
    query_ct_rows, key_value_ct = pullback(query_ct)
    half = feature_width // 2
    onehot_three = jnp.concatenate([query_onehot] * 3, axis=0)
    grad_parts = []
    for part in range(2):
        cols = slice(part * half, (part + 1) * half)
        query_part = lax.dot_general(
            query_ct_rows,
            qkv_full[0][cols],
            (((1,), (1,)), ((), ())),
            preferred_element_type=jnp.float32,
        )
        slot_part = lax.dot_general(
            key_value_ct,
            kv_full[cols],
            (((1,), (1,)), ((), ())),
            preferred_element_type=jnp.float32,
        )
        scatter_src = query_part + query_ct[:, cols]
        piece_hi = lax.reduce_precision(scatter_src, exponent_bits=8, mantissa_bits=7)
        rest = scatter_src - piece_hi
        piece_mid = lax.reduce_precision(rest, exponent_bits=8, mantissa_bits=7)
        piece_lo = rest - piece_mid
        pieces = jnp.concatenate([piece_hi, piece_mid, piece_lo], axis=0).astype(jnp.bfloat16)
        scatter_part = lax.dot_general(
            onehot_three, pieces, (((0,), (0,)), ((), ())), preferred_element_type=jnp.float32
        )
        slot_gradient = (slot_part + scatter_part).astype(jnp.bfloat16)
        back_rows = jnp.einsum(
            "sop,sd->opd", recv_onehot, slot_gradient, preferred_element_type=jnp.float32
        ).astype(jnp.bfloat16)
        home_rows = lax.all_to_all(back_rows, "dp", split_axis=0, concat_axis=0, tiled=True)
        grad_parts.append(
            jnp.einsum(
                "opk,opd->kd", send_onehot, home_rows, preferred_element_type=jnp.float32
            ).astype(jnp.bfloat16)
        )
    page_grad = jnp.concatenate(grad_parts, axis=1)
    return (page_grad, pair_loss)


def solution(mesh):
    return jax.shard_map(
        body,
        mesh=mesh,
        in_specs=(
            P(("dp", "fsdp"), None),
            P(("dp", "fsdp")),
            P(("dp", "fsdp"), None),
            P(None, "fsdp", None),
            P(None, "fsdp"),
            P(("dp", "fsdp")),
            P(("dp", "fsdp")),
            P(),
            P(("dp", "fsdp")),
        ),
        out_specs=(P(("dp", "fsdp"), None), P(("dp", "fsdp"))),
        check_vma=False,
    )
```

profile of v0, /device:TPU:0, one launch (start us, length us, event | category | flops | bytes accessed | tf_op | source)
XLA Modules:
  0.0 259.1 jit_solution(14258695298128781325)
XLA Ops:
  7.2 0.7 all-gather.3.cloned.1.call-update
  7.9 0.7 add_select_fusion.2
  8.7 1.4 reduce-window.6
  10.1 0.2 slice_reduce_fusion
  10.5 0.7 add_select_fusion.1
  11.2 0.3 fusion.14
  11.5 0.3 select_reduce_fusion
  12.0 0.6 compare_reduce_fusion.1
  12.6 0.7 fusion.82
  13.4 0.6 compare_reduce_fusion
  14.1 0.7 broadcast_select_fusion
  14.7 0.4 scatter.15
  15.1 0.4 broadcast_compare_fusion
  15.5 4.5 %add_convert_fusion = bf16[16,51,2048]{2,1,0:T(8,128)(2,1)} fusion(f32[16,1,2048]{2,1,0:T(1,128)S(1)} %scatter.15, bf16[640,2048]{1,0:T(8,128)(2,1)S(1)} %copy-done, pred[16,50,640]{2,1,0:T(8,128)(4,1)S(1)} %broadcast_compare_fusion), kind=kOutput, calls=%fused_computation.6 | convolution fusion | flops 2142437376 | bytes 6606848 | tf_op jit(solution)/shard_map/opk,kd->opd/dot_general | solution.py:87
  20.0 7.3 %all-to-all-start = ((bf16[16,51,2048]{2,1,0:T(8,128)(2,1)}), bf16[16,51,2048]{2,1,0:T(8,128)(2,1)}, u32[]{:S(2)}, u32[]{:S(2)}) async-start(bf16[16,51,2048]{2,1,0:T(8,128)(2,1)} %add_convert_fusion), calls=%async_computation | async-start | bytes 7340032 | tf_op jit(solution)/shard_map/all_to_all | solution.py:90
  27.6 0.5 all-gather.5.cloned.1.call-update
  28.3 0.6 fusion.114
  28.9 1.7 scatter.19
  31.0 46.8 %all-to-all-done = bf16[16,51,2048]{2,1,0:T(8,128)(2,1)} async-done(((bf16[16,51,2048]{2,1,0:T(8,128)(2,1)}), bf16[16,51,2048]{2,1,0:T(8,128)(2,1)}, u32[]{:S(2)}, u32[]{:S(2)}) %all-to-all-start) | async-done | bytes 3342368 | tf_op jit(solution)/shard_map/all_to_all | solution.py:90
  77.8 1.1 slice_convert_fusion
  79.0 5.1 %bitcast_convert_fusion = bf16[640,2048]{1,0:T(8,128)(2,1)S(1)} fusion(bf16[16,51,2048]{2,1,0:T(8,128)(2,1)} %all-to-all-done, s32[16,51]{1,0:T(8,128)S(1)} %concatenate.54), kind=kOutput, calls=%fused_computation.7 | convolution fusion | flops 2140928000 | bytes 5967040 | tf_op jit(solution)/shard_map/sop,opd->sd/dot_general | solution.py:99
  84.1 0.6 convolution_convert_fusion
  84.8 3.0 %fusion.37 = bf16[32,1024]{1,0:T(8,128)(2,1)S(1)} fusion(bf16[32,2048]{1,0:T(8,128)(2,1)S(1)} %convolution_convert_fusion, bf16[3,2048,1024]{2,1,0:T(8,128)(2,1)} %all-gather.3.cloned.1.call-done), kind=kOutput, calls=%fused_computation.71 | convolution fusion | flops 134250496 | bytes 4390912 | tf_op jit(solution)/shard_map/dot_general | solution.py:116
  87.9 4.2 %slice_bitcast_fusion.2 = (bf16[2048,1024]{1,0:T(8,128)(2,1)S(1)}, bf16[2048,1024]{1,0:T(8,128)(2,1)S(1)}) fusion(bf16[3,2048,1024]{2,1,0:T(8,128)(2,1)} %all-gather.3.cloned.1.call-done), kind=kLoop, calls=%fused_computation.14 | loop fusion | bytes 16777216 | tf_op jit(solution)/shard_map/squeeze | solution.py:106
  92.2 6.1 %fusion.8 = bf16[640,2048]{1,0:T(8,128)(2,1)S(1)} fusion(bf16[640,2048]{1,0:T(8,128)(2,1)S(1)} %bitcast_convert_fusion, bf16[2048,1024]{1,0:T(8,128)(2,1)S(1)} %get-tuple-element.57, bf16[2048,1024]{1,0:T(8,128)(2,1)S(1)} %get-tuple-element.58), kind=kOutput, calls=%fused_computation.16 | convolution fusion | flops 5386797056 | bytes 13631488 | tf_op jit(solution)/shard_map/dot_general | solution.py:119
  98.3 0.3 fusion.112
  98.5 1.5 copy.42
  100.0 0.7 copy.43
  100.8 0.5 fusion.115
  101.3 1.8 copy-done.7
  103.0 0.6 fusion.34
  103.9 14.1 %all-gather.5.cloned.1.call-done = bf16[1024,2048]{1,0:T(8,128)(2,1)} async-done(((bf16[1024,256]{1,0:T(8,128)(2,1)}), bf16[1024,2048]{1,0:T(8,128)(2,1)}) %all-gather.5.cloned.1.call-update) | async-done | bytes 4194320 | tf_op jit(solution)/shard_map/all_gather | solution.py:104
  118.0 3.0 %convolution_add_fusion = f32[32,2048]{1,0:T(8,128)S(1)} fusion(bf16[32,1024]{1,0:T(8,128)(2,1)S(1)} %reshape.309, bf16[1024,2048]{1,0:T(8,128)(2,1)} %all-gather.5.cloned.1.call-done, bf16[32,2048]{1,0:T(8,128)(2,1)S(1)} %convolution_convert_fusion), kind=kOutput, calls=%fused_computation.27 | convolution fusion | flops 134348800 | bytes 4653056 | tf_op jit(solution)/shard_map/jvp()/dot_general | solution.py:31
  121.3 1.5 broadcast_in_dim.99
  122.8 6.8 %all-to-all-start.1 = ((bf16[16,32,2176]{2,1,0:T(8,128)(2,1)}), bf16[16,32,2176]{2,1,0:T(8,128)(2,1)S(1)}, u32[]{:S(2)}, u32[]{:S(2)}) async-start(bf16[16,32,2176]{2,1,0:T(8,128)(2,1)} %broadcast_in_dim.99), calls=%async_computation.1 | async-start | bytes 4456448 | tf_op jit(solution)/shard_map/all_to_all | solution.py:141
  130.3 0.7 iota_compare_fusion.10
  131.0 0.6 multiply_divide_fusion
  131.6 30.2 %all-to-all-done.1 = bf16[16,32,2176]{2,1,0:T(8,128)(2,1)S(1)} async-done(((bf16[16,32,2176]{2,1,0:T(8,128)(2,1)}), bf16[16,32,2176]{2,1,0:T(8,128)(2,1)S(1)}, u32[]{:S(2)}, u32[]{:S(2)}) %all-to-all-start.1) | async-done | bytes 2228256 | tf_op jit(solution)/shard_map/all_to_all | solution.py:141
  162.1 0.3 fusion.113
  162.4 0.6 select_reduce_fusion.1
  163.5 0.6 convolution_multiply_fusion
  164.1 0.6 multiply_reduce_fusion.1
  164.9 0.3 copy-done.2
  165.1 1.3 convolution_convert_fusion.6
  166.5 0.8 reshape.316
  167.3 1.7 fusion.26
  169.1 0.6 fusion.33
  169.7 0.3 copy-done.12
  170.0 1.7 convolution_convert_fusion.1
  171.7 1.7 convolution_convert_fusion.2
  173.6 7.4 %fusion.5 = f32[640,1024]{1,0:T(8,128)} fusion(bf16[2048,1024]{1,0:T(8,128)(2,1)} %copy-done.9, bf16[2048,1024]{1,0:T(8,128)(2,1)} %copy-done.8, bf16[640,1024]{0,1:T(8,128)(2,1)} %bitcast.134, bf16[640,1024]{0,1:T(8,128)(2,1)} %bitcast.136), kind=kOutput, calls=%fused_computation.11 | convolution fusion | flops 2697986048 | bytes 13631488 | tf_op jit(solution)/shard_map/dot_general | solution.py:199
  181.1 2.3 reduce-precision_convert_fusion.1
  183.4 5.0 %fusion.16 = bf16[16,51,1024]{2,1,0:T(8,128)(2,1)} fusion(s32[16,51]{1,0:T(8,128)S(1)} %copy-done.18, f32[640,1024]{1,0:T(8,128)} %fusion.5, bf16[32,1024]{1,0:T(8,128)(2,1)S(1)} %get-tuple-element.71, bf16[32,1024]{1,0:T(8,128)(2,1)S(1)} %get-tuple-element.72, bf16[32,1024]{1,0:T(8,128)(2,1)S(1)} %get-tuple-element.70, pred[32,640]{1,0:T(32,128)(4,1)S(1)} %copy-done.16), kind=kOutput, calls=%fused_computation.39 | convolution fusion | flops 1198757888 | bytes 4512960 | tf_op jit(solution)/shard_map/sop,sd->opd/dot_general | solution.py:215
  188.5 5.1 %all-to-all-start.3 = ((bf16[16,51,1024]{2,1,0:T(8,128)(2,1)}), bf16[16,51,1024]{2,1,0:T(8,128)(2,1)S(1)}, u32[]{:S(2)}, u32[]{:S(2)}) async-start(bf16[16,51,1024]{2,1,0:T(8,128)(2,1)} %fusion.16), calls=%async_computation.3 | async-start | bytes 3670016 | tf_op jit(solution)/shard_map/all_to_all | solution.py:218
  193.6 2.5 reduce-precision_convert_fusion.3
  196.1 6.7 %fusion.2 = f32[640,1024]{1,0:T(8,128)} fusion(bf16[2048,1024]{1,0:T(8,128)(2,1)} %copy-done.9, bf16[2048,1024]{1,0:T(8,128)(2,1)} %copy-done.8, bf16[640,1024]{0,1:T(8,128)(2,1)S(1)} %bitcast.135, bf16[640,1024]{0,1:T(8,128)(2,1)S(1)} %bitcast.137), kind=kOutput, calls=%fused_computation.9 | convolution fusion | flops 2697986048 | bytes 13631488 | tf_op jit(solution)/shard_map/dot_general | solution.py:199
  202.8 5.0 %fusion.15 = bf16[16,51,1024]{2,1,0:T(8,128)(2,1)} fusion(s32[16,51]{1,0:T(8,128)S(1)} %copy-done.18, f32[640,1024]{1,0:T(8,128)} %fusion.2, bf16[32,1024]{1,0:T(8,128)(2,1)S(1)} %get-tuple-element.68, bf16[32,1024]{1,0:T(8,128)(2,1)S(1)} %get-tuple-element.69, bf16[32,1024]{1,0:T(8,128)(2,1)S(1)} %get-tuple-element.67, pred[32,640]{1,0:T(32,128)(4,1)S(1)} %copy-done.16), kind=kOutput, calls=%fused_computation.38 | convolution fusion | flops 1198757888 | bytes 4512960 | tf_op jit(solution)/shard_map/sop,sd->opd/dot_general | solution.py:215
  207.8 11.8 %all-to-all-done.3 = bf16[16,51,1024]{2,1,0:T(8,128)(2,1)S(1)} async-done(((bf16[16,51,1024]{2,1,0:T(8,128)(2,1)}), bf16[16,51,1024]{2,1,0:T(8,128)(2,1)S(1)}, u32[]{:S(2)}, u32[]{:S(2)}) %all-to-all-start.3) | async-done | bytes 1671200 | tf_op jit(solution)/shard_map/all_to_all | solution.py:218
  219.6 4.4 %all-to-all-start.2 = ((bf16[16,51,1024]{2,1,0:T(8,128)(2,1)}), bf16[16,51,1024]{2,1,0:T(8,128)(2,1)}, u32[]{:S(2)}, u32[]{:S(2)}) async-start(bf16[16,51,1024]{2,1,0:T(8,128)(2,1)} %fusion.15), calls=%async_computation.2 | async-start | bytes 3670016 | tf_op jit(solution)/shard_map/all_to_all | solution.py:218
  224.0 0.7 convolution_bitcast_fusion
  224.7 2.7 %bitcast_convert_fusion.1 = bf16[640,1024]{1,0:T(8,128)(2,1)} fusion(bf16[16,51,1024]{2,1,0:T(8,128)(2,1)S(1)} %all-to-all-done.3, pred[16,50,640]{2,1,0:T(8,128)(4,1)S(1)} %broadcast_compare_fusion), kind=kOutput, calls=%fused_computation.18 | convolution fusion | flops 1070202880 | bytes 3493888 | tf_op jit(solution)/shard_map/opk,opd->kd/dot_general | solution.py:220
  227.4 19.8 %all-to-all-done.2 = bf16[16,51,1024]{2,1,0:T(8,128)(2,1)} async-done(((bf16[16,51,1024]{2,1,0:T(8,128)(2,1)}), bf16[16,51,1024]{2,1,0:T(8,128)(2,1)}, u32[]{:S(2)}, u32[]{:S(2)}) %all-to-all-start.2) | async-done | bytes 1671200 | tf_op jit(solution)/shard_map/all_to_all | solution.py:218
  247.2 3.3 %bitcast_convert_fusion.2 = bf16[640,1024]{1,0:T(8,128)(2,1)S(1)} fusion(bf16[16,51,1024]{2,1,0:T(8,128)(2,1)} %all-to-all-done.2, pred[16,50,640]{2,1,0:T(8,128)(4,1)S(1)} %broadcast_compare_fusion), kind=kOutput, calls=%fused_computation.19 | convolution fusion | flops 1070202880 | bytes 3493888 | tf_op jit(solution)/shard_map/opk,opd->kd/dot_general | solution.py:220
  250.5 1.7 pad_maximum_fusion.4
  (93 shorter events, 3.2 us)
Async XLA Ops:
  7.2 8.4 %copy-start = (bf16[640,2048]{1,0:T(8,128)(2,1)S(1)}, bf16[640,2048]{1,0:T(8,128)(2,1)}, u32[]{:S(2)}) copy-start(bf16[640,2048]{1,0:T(8,128)(2,1)} %param.17) | copy-start | bytes 7864324
  7.2 77.6 %all-gather.3.cloned.1.call-start = ((), (), s32[]{:S(2)}) async-start(), calls=%async_computation.4 | async-start | bytes 14155776 | tf_op jit(solution)/shard_map/all_gather | solution.py:103
  20.0 8.1 %copy-start.22 = (f32[16]{0:T(128)S(1)}, f32[16]{0:T(128)}, u32[]{:S(2)}) copy-start(f32[16]{0:T(128)} %param.25) | copy-start | bytes 196
  20.0 8.2 %copy-start.19 = (s32[1,640]{1,0:T(1,128)S(1)}, s32[1,640]{1,0:T(1,128)}, u32[]{:S(2)}) copy-start(s32[1,640]{1,0:T(1,128)} %param.19) | copy-start | bytes 7684
  20.0 10.6 %copy-start.23 = (s32[16]{0:T(128)S(1)}, s32[16]{0:T(128)}, u32[]{:S(2)}) copy-start(s32[16]{0:T(128)} %param.23) | copy-start | bytes 196
  20.0 10.6 %copy-start.24 = (s32[16]{0:T(128)S(1)}, s32[16]{0:T(128)}, u32[]{:S(2)}) copy-start(s32[16]{0:T(128)} %param.22) | copy-start | bytes 196
  20.0 57.8 %all-to-all-start = ((bf16[16,51,2048]{2,1,0:T(8,128)(2,1)}), bf16[16,51,2048]{2,1,0:T(8,128)(2,1)}, u32[]{:S(2)}, u32[]{:S(2)}) async-start(bf16[16,51,2048]{2,1,0:T(8,128)(2,1)} %add_convert_fusion), calls=%async_computation | async-start | bytes 7340032 | tf_op jit(solution)/shard_map/all_to_all | solution.py:90
  27.3 90.7 %all-gather.5.cloned.1.call-start = ((), (), s32[]{:S(2)}) async-start(), calls=%async_computation.5 | async-start | bytes 4718592 | tf_op jit(solution)/shard_map/all_gather | solution.py:104
  30.6 48.4 %copy-start.14 = (bf16[32,128]{1,0:T(8,128)(2,1)}, bf16[32,128]{1,0:T(8,128)(2,1)S(1)}, u32[]{:S(2)}) copy-start(bf16[32,128]{1,0:T(8,128)(2,1)S(1)} %scatter.19) | copy-start | bytes 24580
  79.0 5.1 %copy-start.17 = (s32[16,51]{1,0:T(8,128)}, s32[16,51]{1,0:T(8,128)S(1)}, u32[]{:S(2)}) copy-start(s32[16,51]{1,0:T(8,128)S(1)} %concatenate.54) | copy-start | bytes 9796
  87.9 12.8 %copy-start.11 = (bf16[32,16,64]{2,1,0:T(8,128)(2,1)}, bf16[32,16,64]{2,1,0:T(8,128)(2,1)S(1)}, u32[]{:S(2)}) copy-start(bf16[32,16,64]{2,1,0:T(8,128)(2,1)S(1)} %reshape.307) | copy-start | bytes 196612
  92.1 6.1 %copy-start.8 = (bf16[2048,1024]{1,0:T(8,128)(2,1)}, bf16[2048,1024]{1,0:T(8,128)(2,1)S(1)}, u32[]{:S(2)}) copy-start(bf16[2048,1024]{1,0:T(8,128)(2,1)S(1)} %get-tuple-element.57) | copy-start | bytes 12582916
  92.1 6.1 %copy-start.9 = (bf16[2048,1024]{1,0:T(8,128)(2,1)}, bf16[2048,1024]{1,0:T(8,128)(2,1)S(1)}, u32[]{:S(2)}) copy-start(bf16[2048,1024]{1,0:T(8,128)(2,1)S(1)} %get-tuple-element.58) | copy-start | bytes 12582916
  100.7 2.9 %copy-start.5 = (bf16[640,1024]{0,1:T(8,128)(2,1)}, bf16[640,1024]{0,1:T(8,128)(2,1)S(1)}, u32[]{:S(2)}) copy-start(bf16[640,1024]{0,1:T(8,128)(2,1)S(1)} %copy.43) | copy-start | bytes 3932164
  100.7 2.3 copy-start.7
  101.3 2.4 copy-start.3
  103.9 17.4 %copy-start.15 = (bf16[32,128]{1,0:T(8,128)(2,1)S(1)}, bf16[32,128]{1,0:T(8,128)(2,1)}, u32[]{:S(2)}) copy-start(bf16[32,128]{1,0:T(8,128)(2,1)} %copy-done.14) | copy-start | bytes 24580
  122.8 39.0 %all-to-all-start.1 = ((bf16[16,32,2176]{2,1,0:T(8,128)(2,1)}), bf16[16,32,2176]{2,1,0:T(8,128)(2,1)S(1)}, u32[]{:S(2)}, u32[]{:S(2)}) async-start(bf16[16,32,2176]{2,1,0:T(8,128)(2,1)} %broadcast_in_dim.99), calls=%async_computation.1 | async-start | bytes 4456448 | tf_op jit(solution)/shard_map/all_to_all | solution.py:141
  130.3 33.0 %copy-start.20 = (s32[16]{0:T(128)}, s32[16]{0:T(128)S(1)}, u32[]{:S(2)}) copy-start(s32[16]{0:T(128)S(1)} %iota_add_fusion) | copy-start | bytes 196
  162.9 2.2 copy-start.2
  164.8 2.5 copy-start.4
  166.5 2.6 %copy-start.6 = (bf16[640,1024]{0,1:T(8,128)(2,1)S(1)}, bf16[640,1024]{0,1:T(8,128)(2,1)}, u32[]{:S(2)}) copy-start(bf16[640,1024]{0,1:T(8,128)(2,1)} %copy-done.5) | copy-start | bytes 3932164
  169.1 0.9 copy-start.12
  170.0 1.7 copy-start.13
  181.1 2.4 copy-start.16
  181.1 2.4 copy-start.18
  188.5 31.1 %all-to-all-start.3 = ((bf16[16,51,1024]{2,1,0:T(8,128)(2,1)}), bf16[16,51,1024]{2,1,0:T(8,128)(2,1)S(1)}, u32[]{:S(2)}, u32[]{:S(2)}) async-start(bf16[16,51,1024]{2,1,0:T(8,128)(2,1)} %fusion.16), calls=%async_computation.3 | async-start | bytes 3670016 | tf_op jit(solution)/shard_map/all_to_all | solution.py:218
  193.6 2.5 copy-start.25
  193.6 2.5 copy-start.26
  207.8 16.2 %copy-start.21 = (s32[16]{0:T(128)S(1)}, s32[16]{0:T(128)}, u32[]{:S(2)}) copy-start(s32[16]{0:T(128)} %copy-done.20) | copy-start | bytes 196
  219.6 27.6 %all-to-all-start.2 = ((bf16[16,51,1024]{2,1,0:T(8,128)(2,1)}), bf16[16,51,1024]{2,1,0:T(8,128)(2,1)}, u32[]{:S(2)}, u32[]{:S(2)}) async-start(bf16[16,51,1024]{2,1,0:T(8,128)(2,1)} %fusion.15), calls=%async_computation.2 | async-start | bytes 3670016 | tf_op jit(solution)/shard_map/all_to_all | solution.py:218
  247.2 3.3 %copy-start.10 = (bf16[640,1024]{1,0:T(8,128)(2,1)S(1)}, bf16[640,1024]{1,0:T(8,128)(2,1)}, u32[]{:S(2)}) copy-start(bf16[640,1024]{1,0:T(8,128)(2,1)} %bitcast_convert_fusion.1) | copy-start | bytes 3932164
  247.2 5.0 %copy-start.1 = (bf16[640,2048]{1,0:T(8,128)(2,1)S(1)}, bf16[640,2048]{1,0:T(8,128)(2,1)}, u32[]{:S(2)}) copy-start(bf16[640,2048]{1,0:T(8,128)(2,1)} %param.17) | copy-start | bytes 7864324
Sparse Core Ops, SparseCore 0:
  9.7 69.9 all-gather.2
  81.4 36.5 all-gather.4
where the time goes:
time: 260 us; the launch traced here: 259 us
  waiting for transfers between devices  124 us (48%)
  matrix products  68.3 us (26%)
  starting transfers between devices  23.9 us (9%)
  local copies, waits for them, and re-layouts  15.7 us (6%)
  between operations  15.3 us (6%)
  other arithmetic  11.9 us (5%)
    all_to_all x1, waiting for transfers between devices, body(): lax.all_to_all(send_rows, 'dp', split_axis=0, concat_axis=0, tiled=True)  46.8 us
    all_to_all x2, waiting for transfers between devices, body(): lax.all_to_all(back_rows, 'dp', split_axis=0, concat_axis=0, tiled=True)  31.6 us
    all_to_all x1, waiting for transfers between devices, body(): lax.all_to_all(jnp.broadcast_to(both_emb[None], (dp_count,) + both_emb.sh...  30.2 us
    dot_general x2, matrix products, body(): lax.dot_general(key_value_ct, kv_full[cols], (((1,), (1,)), ((), ())), pr...  14.1 us
    all_gather x1, waiting for transfers between devices, body(): lax.all_gather(out_weight, 'fsdp', axis=1, tiled=True)  14.1 us
    dot_general x2, matrix products, body(): jnp.einsum('sop,sd->opd', recv_onehot, slot_gradient, preferred_element_t...  10 us
    all_to_all x2, starting transfers between devices, body(): lax.all_to_all(back_rows, 'dp', split_axis=0, concat_axis=0, tiled=True)  9.51 us
    all_to_all x1, starting transfers between devices, body(): lax.all_to_all(send_rows, 'dp', split_axis=0, concat_axis=0, tiled=True)  7.3 us
  transfers between devices with their start and end apart: 6, of which 5 were waited for; matrix products, arithmetic and copies ran while one was open for 22% of the time, Pallas kernels for 0%

commit v1 on v0

--- a/solution.py
+++ b/solution.py
@@ -101,7 +101,9 @@
     ).astype(jnp.bfloat16)
     qkv_full, out_full = (
         lax.all_gather(qkv_weight, "fsdp", axis=1, tiled=True),
-        lax.all_gather(out_weight, "fsdp", axis=1, tiled=True),
+        jnp.concatenate(
+            lax.all_to_all(jnp.stack([out_weight] * lax.axis_size("fsdp")), "fsdp", 0, 0), axis=1
+        ),
     )
     kv_full = jnp.concatenate([qkv_full[1], qkv_full[2]], axis=1)
     doc_row = doc_ids[0]

time: 260 us -> 281 us (1.081)
  starting transfers between devices: 23.9 us -> 32.7 us
  waiting for transfers between devices: 124 us -> 131 us
    all_to_all x0 -> x1, waiting for transfers between devices: none -> 24 us  [body(): lax.all_to_all(jnp.stack([out_weight] * lax.axis_size('fsdp')), 'fsdp', 0...]
    all_gather x1 -> x0, waiting for transfers between devices: 14.1 us -> none  [body(): lax.all_gather(out_weight, 'fsdp', axis=1, tiled=True)]
    all_to_all x0 -> x1, starting transfers between devices: none -> 5.27 us  [body(): lax.all_to_all(jnp.stack([out_weight] * lax.axis_size('fsdp')), 'fsdp', 0...]
    all_to_all x1, starting transfers between devices: 6.81 us -> 11.7 us  [body(): lax.all_to_all(jnp.broadcast_to(both_emb[None], (dp_count,) + both_emb.sh...]
where the time goes in v1:
time: 281 us; the launch traced here: 280 us
  waiting for transfers between devices  131 us (47%)
  matrix products  70.6 us (25%)
  starting transfers between devices  32.7 us (12%)
  local copies, waits for them, and re-layouts  17.9 us (6%)
  between operations  15.4 us (5%)
  other arithmetic  11.9 us (4%)
    all_to_all x1, waiting for transfers between devices, body(): lax.all_to_all(send_rows, 'dp', split_axis=0, concat_axis=0, tiled=True)  47.3 us
    all_to_all x1, waiting for transfers between devices, body(): lax.all_to_all(jnp.broadcast_to(both_emb[None], (dp_count,) + both_emb.sh...  29.7 us
    all_to_all x2, waiting for transfers between devices, body(): lax.all_to_all(back_rows, 'dp', split_axis=0, concat_axis=0, tiled=True)  29.6 us
    all_to_all x1, waiting for transfers between devices, body(): lax.all_to_all(jnp.stack([out_weight] * lax.axis_size('fsdp')), 'fsdp', 0...  24 us
    dot_general x2, matrix products, body(): lax.dot_general(key_value_ct, kv_full[cols], (((1,), (1,)), ((), ())), pr...  14.1 us
    all_to_all x1, starting transfers between devices, body(): lax.all_to_all(jnp.broadcast_to(both_emb[None], (dp_count,) + both_emb.sh...  11.7 us
    dot_general x2, matrix products, body(): jnp.einsum('sop,sd->opd', recv_onehot, slot_gradient, preferred_element_t...  10 us
    all_to_all x2, starting transfers between devices, body(): lax.all_to_all(back_rows, 'dp', split_axis=0, concat_axis=0, tiled=True)  8.4 us
  transfers between devices with their start and end apart: 6, of which 5 were waited for; matrix products, arithmetic and copies ran while one was open for 22% of the time, Pallas kernels for 0%

profile of v1, /device:TPU:0, one launch (start us, length us, event | category | flops | bytes accessed | tf_op | source)
XLA Modules:
  0.0 279.7 jit_solution(1242019183952692527)
XLA Ops:
  7.2 0.7 all-gather.2.cloned.1.call-update
  7.9 0.7 add_select_fusion.2
  8.7 1.4 reduce-window.6
  10.1 0.2 slice_reduce_fusion
  10.5 0.7 add_select_fusion.1
  11.2 0.3 fusion.14
  11.5 0.3 select_reduce_fusion
  12.0 0.6 compare_reduce_fusion.1
  12.6 0.7 fusion.82
  13.4 0.6 compare_reduce_fusion
  14.1 0.7 broadcast_select_fusion
  14.7 0.4 scatter.15
  15.1 0.4 broadcast_compare_fusion
  15.5 4.5 %add_convert_fusion = bf16[16,51,2048]{2,1,0:T(8,128)(2,1)} fusion(f32[16,1,2048]{2,1,0:T(1,128)S(1)} %scatter.15, bf16[640,2048]{1,0:T(8,128)(2,1)S(1)} %copy-done, pred[16,50,640]{2,1,0:T(8,128)(4,1)S(1)} %broadcast_compare_fusion), kind=kOutput, calls=%fused_computation.6 | convolution fusion | flops 2142437376 | bytes 6606848 | tf_op jit(solution)/shard_map/opk,kd->opd/dot_general | solution.py:87
  20.0 7.3 %all-to-all-start = ((bf16[16,51,2048]{2,1,0:T(8,128)(2,1)}), bf16[16,51,2048]{2,1,0:T(8,128)(2,1)}, u32[]{:S(2)}, u32[]{:S(2)}) async-start(bf16[16,51,2048]{2,1,0:T(8,128)(2,1)} %add_convert_fusion), calls=%async_computation | async-start | bytes 7340032 | tf_op jit(solution)/shard_map/all_to_all | solution.py:90
  27.8 0.6 fusion.114
  28.4 1.7 scatter.19
  30.5 47.3 %all-to-all-done = bf16[16,51,2048]{2,1,0:T(8,128)(2,1)} async-done(((bf16[16,51,2048]{2,1,0:T(8,128)(2,1)}), bf16[16,51,2048]{2,1,0:T(8,128)(2,1)}, u32[]{:S(2)}, u32[]{:S(2)}) %all-to-all-start) | async-done | bytes 3342368 | tf_op jit(solution)/shard_map/all_to_all | solution.py:90
  77.8 2.5 stack.2
  80.3 5.3 %all-to-all-start.1 = ((bf16[8,1024,256]{1,2,0:T(8,128)(2,1)}), bf16[8,1024,256]{1,2,0:T(8,128)(2,1)}, u32[]{:S(2)}, u32[]{:S(2)}) async-start(bf16[8,1024,256]{1,2,0:T(8,128)(2,1)} %stack.2), calls=%async_computation.1 | async-start | bytes 8388608 | tf_op jit(solution)/shard_map/all_to_all | solution.py:105
  85.6 1.1 slice_convert_fusion
  86.8 5.1 %bitcast_convert_fusion = bf16[640,2048]{1,0:T(8,128)(2,1)S(1)} fusion(bf16[16,51,2048]{2,1,0:T(8,128)(2,1)} %all-to-all-done, s32[16,51]{1,0:T(8,128)S(1)} %concatenate.54), kind=kOutput, calls=%fused_computation.7 | convolution fusion | flops 2140928000 | bytes 5967040 | tf_op jit(solution)/shard_map/sop,opd->sd/dot_general | solution.py:99
  91.9 0.6 convolution_convert_fusion
  92.5 3.0 %fusion.37 = bf16[32,1024]{1,0:T(8,128)(2,1)S(1)} fusion(bf16[32,2048]{1,0:T(8,128)(2,1)S(1)} %convolution_convert_fusion, bf16[3,2048,1024]{2,1,0:T(8,128)(2,1)} %all-gather.2.cloned.1.call-done), kind=kOutput, calls=%fused_computation.71 | convolution fusion | flops 134250496 | bytes 4390912 | tf_op jit(solution)/shard_map/dot_general | solution.py:118
  95.7 4.0 %slice_bitcast_fusion.2 = (bf16[2048,1024]{1,0:T(8,128)(2,1)S(1)}, bf16[2048,1024]{1,0:T(8,128)(2,1)S(1)}) fusion(bf16[3,2048,1024]{2,1,0:T(8,128)(2,1)} %all-gather.2.cloned.1.call-done), kind=kLoop, calls=%fused_computation.14 | loop fusion | bytes 16777216 | tf_op jit(solution)/shard_map/squeeze | solution.py:108
  99.7 6.1 %fusion.8 = bf16[640,2048]{1,0:T(8,128)(2,1)S(1)} fusion(bf16[640,2048]{1,0:T(8,128)(2,1)S(1)} %bitcast_convert_fusion, bf16[2048,1024]{1,0:T(8,128)(2,1)S(1)} %get-tuple-element.57, bf16[2048,1024]{1,0:T(8,128)(2,1)S(1)} %get-tuple-element.58), kind=kOutput, calls=%fused_computation.16 | convolution fusion | flops 5386797056 | bytes 13631488 | tf_op jit(solution)/shard_map/dot_general | solution.py:121
  105.8 0.3 fusion.112
  106.1 1.5 copy.44
  107.6 0.7 copy.45
  108.3 0.5 fusion.115
  108.8 1.7 copy-done.6
  110.6 0.6 fusion.34
  111.4 24.0 %all-to-all-done.1 = bf16[8,1024,256]{1,2,0:T(8,128)(2,1)} async-done(((bf16[8,1024,256]{1,2,0:T(8,128)(2,1)}), bf16[8,1024,256]{1,2,0:T(8,128)(2,1)}, u32[]{:S(2)}, u32[]{:S(2)}) %all-to-all-start.1) | async-done | bytes 4194336 | tf_op jit(solution)/shard_map/all_to_all | solution.py:105
  135.4 3.5 %convolution_add_fusion = f32[32,2048]{1,0:T(8,128)S(1)} fusion(bf16[32,1024]{1,0:T(8,128)(2,1)S(1)} %reshape.317, bf16[1024,2048]{0,1:T(8,128)(2,1)} %bitcast.11, bf16[32,2048]{1,0:T(8,128)(2,1)S(1)} %convolution_convert_fusion), kind=kOutput, calls=%fused_computation.27 | convolution fusion | flops 134348800 | bytes 4653056 | tf_op jit(solution)/shard_map/jvp()/dot_general | solution.py:31
  139.2 1.5 broadcast_in_dim.99
  140.7 11.7 %all-to-all-start.2 = ((bf16[16,32,2176]{2,1,0:T(8,128)(2,1)}), bf16[16,32,2176]{2,1,0:T(8,128)(2,1)S(1)}, u32[]{:S(2)}, u32[]{:S(2)}) async-start(bf16[16,32,2176]{2,1,0:T(8,128)(2,1)} %broadcast_in_dim.99), calls=%async_computation.2 | async-start | bytes 4456448 | tf_op jit(solution)/shard_map/all_to_all | solution.py:143
  153.1 0.7 iota_compare_fusion.10
  153.7 0.6 multiply_divide_fusion
  154.3 29.7 %all-to-all-done.2 = bf16[16,32,2176]{2,1,0:T(8,128)(2,1)S(1)} async-done(((bf16[16,32,2176]{2,1,0:T(8,128)(2,1)}), bf16[16,32,2176]{2,1,0:T(8,128)(2,1)S(1)}, u32[]{:S(2)}, u32[]{:S(2)}) %all-to-all-start.2) | async-done | bytes 2228256 | tf_op jit(solution)/shard_map/all_to_all | solution.py:143
  184.3 0.3 fusion.113
  184.6 0.6 select_reduce_fusion.1
  185.7 0.6 convolution_multiply_fusion
  186.3 0.6 multiply_reduce_fusion.1
  187.1 3.1 %convolution_convert_fusion.6 = bf16[32,1024]{1,0:T(8,128)(2,1)S(1)} fusion(bf16[1024,2048]{0,1:T(8,128)(2,1)} %bitcast.11, f32[16,2048]{1,0:T(8,128)S(1)} %get-tuple-element.64, f32[16,2048]{1,0:T(8,128)S(1)} %get-tuple-element.63), kind=kOutput, calls=%fused_computation.72 | convolution fusion | flops 134479872 | bytes 4521984 | tf_op jit(solution)/shard_map/transpose(jvp())/dot_general | solution.py:31
  190.2 0.8 reshape.326
  191.0 1.7 fusion.26
  192.8 0.6 fusion.33
  193.4 0.3 copy-done.11
  193.7 1.7 convolution_convert_fusion.1
  195.4 1.7 convolution_convert_fusion.2
  197.3 7.4 %fusion.5 = f32[640,1024]{1,0:T(8,128)} fusion(bf16[2048,1024]{1,0:T(8,128)(2,1)} %copy-done.8, bf16[2048,1024]{1,0:T(8,128)(2,1)} %copy-done.7, bf16[640,1024]{0,1:T(8,128)(2,1)} %bitcast.137, bf16[640,1024]{0,1:T(8,128)(2,1)} %bitcast.139), kind=kOutput, calls=%fused_computation.11 | convolution fusion | flops 2697986048 | bytes 13631488 | tf_op jit(solution)/shard_map/dot_general | solution.py:201
  204.8 2.3 reduce-precision_convert_fusion.1
  207.1 5.0 %fusion.16 = bf16[16,51,1024]{2,1,0:T(8,128)(2,1)} fusion(s32[16,51]{1,0:T(8,128)S(1)} %copy-done.18, f32[640,1024]{1,0:T(8,128)} %fusion.5, bf16[32,1024]{1,0:T(8,128)(2,1)S(1)} %get-tuple-element.71, bf16[32,1024]{1,0:T(8,128)(2,1)S(1)} %get-tuple-element.72, bf16[32,1024]{1,0:T(8,128)(2,1)S(1)} %get-tuple-element.70, pred[32,640]{1,0:T(32,128)(4,1)S(1)} %copy-done.16), kind=kOutput, calls=%fused_computation.39 | convolution fusion | flops 1198757888 | bytes 4512960 | tf_op jit(solution)/shard_map/sop,sd->opd/dot_general | solution.py:217
  212.2 4.0 %all-to-all-start.4 = ((bf16[16,51,1024]{2,1,0:T(8,128)(2,1)}), bf16[16,51,1024]{2,1,0:T(8,128)(2,1)S(1)}, u32[]{:S(2)}, u32[]{:S(2)}) async-start(bf16[16,51,1024]{2,1,0:T(8,128)(2,1)} %fusion.16), calls=%async_computation.4 | async-start | bytes 3670016 | tf_op jit(solution)/shard_map/all_to_all | solution.py:220
  216.2 2.5 reduce-precision_convert_fusion.3
  218.7 6.7 %fusion.2 = f32[640,1024]{1,0:T(8,128)} fusion(bf16[2048,1024]{1,0:T(8,128)(2,1)} %copy-done.8, bf16[2048,1024]{1,0:T(8,128)(2,1)} %copy-done.7, bf16[640,1024]{0,1:T(8,128)(2,1)S(1)} %bitcast.138, bf16[640,1024]{0,1:T(8,128)(2,1)S(1)} %bitcast.140), kind=kOutput, calls=%fused_computation.9 | convolution fusion | flops 2697986048 | bytes 13631488 | tf_op jit(solution)/shard_map/dot_general | solution.py:201
  225.4 5.0 %fusion.15 = bf16[16,51,1024]{2,1,0:T(8,128)(2,1)} fusion(s32[16,51]{1,0:T(8,128)S(1)} %copy-done.18, f32[640,1024]{1,0:T(8,128)} %fusion.2, bf16[32,1024]{1,0:T(8,128)(2,1)S(1)} %get-tuple-element.68, bf16[32,1024]{1,0:T(8,128)(2,1)S(1)} %get-tuple-element.69, bf16[32,1024]{1,0:T(8,128)(2,1)S(1)} %get-tuple-element.67, pred[32,640]{1,0:T(32,128)(4,1)S(1)} %copy-done.16), kind=kOutput, calls=%fused_computation.38 | convolution fusion | flops 1198757888 | bytes 4512960 | tf_op jit(solution)/shard_map/sop,sd->opd/dot_general | solution.py:217
  230.4 9.7 %all-to-all-done.4 = bf16[16,51,1024]{2,1,0:T(8,128)(2,1)S(1)} async-done(((bf16[16,51,1024]{2,1,0:T(8,128)(2,1)}), bf16[16,51,1024]{2,1,0:T(8,128)(2,1)S(1)}, u32[]{:S(2)}, u32[]{:S(2)}) %all-to-all-start.4) | async-done | bytes 1671200 | tf_op jit(solution)/shard_map/all_to_all | solution.py:220
  240.1 4.4 %all-to-all-start.3 = ((bf16[16,51,1024]{2,1,0:T(8,128)(2,1)}), bf16[16,51,1024]{2,1,0:T(8,128)(2,1)}, u32[]{:S(2)}, u32[]{:S(2)}) async-start(bf16[16,51,1024]{2,1,0:T(8,128)(2,1)} %fusion.15), calls=%async_computation.3 | async-start | bytes 3670016 | tf_op jit(solution)/shard_map/all_to_all | solution.py:220
  244.5 0.7 convolution_bitcast_fusion
  245.3 2.7 bitcast_convert_fusion.1
  247.9 19.9 %all-to-all-done.3 = bf16[16,51,1024]{2,1,0:T(8,128)(2,1)} async-done(((bf16[16,51,1024]{2,1,0:T(8,128)(2,1)}), bf16[16,51,1024]{2,1,0:T(8,128)(2,1)}, u32[]{:S(2)}, u32[]{:S(2)}) %all-to-all-start.3) | async-done | bytes 1671200 | tf_op jit(solution)/shard_map/all_to_all | solution.py:220
  267.8 3.3 %bitcast_convert_fusion.2 = bf16[640,1024]{1,0:T(8,128)(2,1)S(1)} fusion(bf16[16,51,1024]{2,1,0:T(8,128)(2,1)} %all-to-all-done.3, pred[16,50,640]{2,1,0:T(8,128)(4,1)S(1)} %broadcast_compare_fusion), kind=kOutput, calls=%fused_computation.19 | convolution fusion | flops 1070202880 | bytes 3493888 | tf_op jit(solution)/shard_map/opk,opd->kd/dot_general | solution.py:222
  271.1 1.7 pad_maximum_fusion.4
  (94 shorter events, 3.2 us)
Async XLA Ops:
  7.2 8.4 %copy-start = (bf16[640,2048]{1,0:T(8,128)(2,1)S(1)}, bf16[640,2048]{1,0:T(8,128)(2,1)}, u32[]{:S(2)}) copy-start(bf16[640,2048]{1,0:T(8,128)(2,1)} %param.17) | copy-start | bytes 7864324
  7.2 85.4 %all-gather.2.cloned.1.call-start = ((), (), s32[]{:S(2)}) async-start(), calls=%async_computation.5 | async-start | bytes 14155776 | tf_op jit(solution)/shard_map/all_gather | solution.py:103
  20.0 7.3 %copy-start.22 = (f32[16]{0:T(128)S(1)}, f32[16]{0:T(128)}, u32[]{:S(2)}) copy-start(f32[16]{0:T(128)} %param.25) | copy-start | bytes 196
  20.0 7.5 %copy-start.19 = (s32[1,640]{1,0:T(1,128)S(1)}, s32[1,640]{1,0:T(1,128)}, u32[]{:S(2)}) copy-start(s32[1,640]{1,0:T(1,128)} %param.19) | copy-start | bytes 7684
  20.0 7.6 %copy-start.12 = (bf16[1024,256]{1,0:T(8,128)(2,1)S(1)}, bf16[1024,256]{1,0:T(8,128)(2,1)}, u32[]{:S(2)}) copy-start(bf16[1024,256]{1,0:T(8,128)(2,1)} %param.21) | copy-start | bytes 1572868
  20.0 10.1 %copy-start.23 = (s32[16]{0:T(128)S(1)}, s32[16]{0:T(128)}, u32[]{:S(2)}) copy-start(s32[16]{0:T(128)} %param.23) | copy-start | bytes 196
  20.0 10.1 %copy-start.24 = (s32[16]{0:T(128)S(1)}, s32[16]{0:T(128)}, u32[]{:S(2)}) copy-start(s32[16]{0:T(128)} %param.22) | copy-start | bytes 196
  20.0 57.8 %all-to-all-start = ((bf16[16,51,2048]{2,1,0:T(8,128)(2,1)}), bf16[16,51,2048]{2,1,0:T(8,128)(2,1)}, u32[]{:S(2)}, u32[]{:S(2)}) async-start(bf16[16,51,2048]{2,1,0:T(8,128)(2,1)} %add_convert_fusion), calls=%async_computation | async-start | bytes 7340032 | tf_op jit(solution)/shard_map/all_to_all | solution.py:90
  30.1 50.2 %copy-start.14 = (bf16[32,128]{1,0:T(8,128)(2,1)}, bf16[32,128]{1,0:T(8,128)(2,1)S(1)}, u32[]{:S(2)}) copy-start(bf16[32,128]{1,0:T(8,128)(2,1)S(1)} %scatter.19) | copy-start | bytes 24580
  80.3 55.0 %all-to-all-start.1 = ((bf16[8,1024,256]{1,2,0:T(8,128)(2,1)}), bf16[8,1024,256]{1,2,0:T(8,128)(2,1)}, u32[]{:S(2)}, u32[]{:S(2)}) async-start(bf16[8,1024,256]{1,2,0:T(8,128)(2,1)} %stack.2), calls=%async_computation.1 | async-start | bytes 8388608 | tf_op jit(solution)/shard_map/all_to_all | solution.py:105
  86.8 5.1 %copy-start.17 = (s32[16,51]{1,0:T(8,128)}, s32[16,51]{1,0:T(8,128)S(1)}, u32[]{:S(2)}) copy-start(s32[16,51]{1,0:T(8,128)S(1)} %concatenate.54) | copy-start | bytes 9796
  95.7 12.6 %copy-start.10 = (bf16[32,16,64]{2,1,0:T(8,128)(2,1)}, bf16[32,16,64]{2,1,0:T(8,128)(2,1)S(1)}, u32[]{:S(2)}) copy-start(bf16[32,16,64]{2,1,0:T(8,128)(2,1)S(1)} %reshape.315) | copy-start | bytes 196612
  99.7 6.1 %copy-start.7 = (bf16[2048,1024]{1,0:T(8,128)(2,1)}, bf16[2048,1024]{1,0:T(8,128)(2,1)S(1)}, u32[]{:S(2)}) copy-start(bf16[2048,1024]{1,0:T(8,128)(2,1)S(1)} %get-tuple-element.57) | copy-start | bytes 12582916
  99.7 6.1 %copy-start.8 = (bf16[2048,1024]{1,0:T(8,128)(2,1)}, bf16[2048,1024]{1,0:T(8,128)(2,1)S(1)}, u32[]{:S(2)}) copy-start(bf16[2048,1024]{1,0:T(8,128)(2,1)S(1)} %get-tuple-element.58) | copy-start | bytes 12582916
  108.3 2.9 %copy-start.4 = (bf16[640,1024]{0,1:T(8,128)(2,1)}, bf16[640,1024]{0,1:T(8,128)(2,1)S(1)}, u32[]{:S(2)}) copy-start(bf16[640,1024]{0,1:T(8,128)(2,1)S(1)} %copy.45) | copy-start | bytes 3932164
  108.3 2.3 copy-start.6
  108.8 2.4 copy-start.2
  135.4 3.8 %copy-start.15 = (bf16[32,128]{1,0:T(8,128)(2,1)S(1)}, bf16[32,128]{1,0:T(8,128)(2,1)}, u32[]{:S(2)}) copy-start(bf16[32,128]{1,0:T(8,128)(2,1)} %copy-done.14) | copy-start | bytes 24580
  140.7 43.3 %all-to-all-start.2 = ((bf16[16,32,2176]{2,1,0:T(8,128)(2,1)}), bf16[16,32,2176]{2,1,0:T(8,128)(2,1)S(1)}, u32[]{:S(2)}, u32[]{:S(2)}) async-start(bf16[16,32,2176]{2,1,0:T(8,128)(2,1)} %broadcast_in_dim.99), calls=%async_computation.2 | async-start | bytes 4456448 | tf_op jit(solution)/shard_map/all_to_all | solution.py:143
  153.1 32.5 %copy-start.20 = (s32[16]{0:T(128)}, s32[16]{0:T(128)S(1)}, u32[]{:S(2)}) copy-start(s32[16]{0:T(128)S(1)} %iota_add_fusion) | copy-start | bytes 196
  187.0 4.0 %copy-start.3 = (f32[16,32,640]{2,1,0:T(8,128)S(1)}, f32[16,32,640]{2,1,0:T(8,128)}, u32[]{:S(2)}) copy-start(f32[16,32,640]{2,1,0:T(8,128)} %copy-done.2) | copy-start | bytes 3932164
  190.2 2.6 copy-start.5
  192.8 0.9 copy-start.11
  193.7 1.7 copy-start.13
  204.8 2.4 copy-start.16
  204.8 2.4 copy-start.18
  212.2 28.0 %all-to-all-start.4 = ((bf16[16,51,1024]{2,1,0:T(8,128)(2,1)}), bf16[16,51,1024]{2,1,0:T(8,128)(2,1)S(1)}, u32[]{:S(2)}, u32[]{:S(2)}) async-start(bf16[16,51,1024]{2,1,0:T(8,128)(2,1)} %fusion.16), calls=%async_computation.4 | async-start | bytes 3670016 | tf_op jit(solution)/shard_map/all_to_all | solution.py:220
  216.2 2.5 copy-start.25
  216.2 2.5 copy-start.26
  230.4 14.2 %copy-start.21 = (s32[16]{0:T(128)S(1)}, s32[16]{0:T(128)}, u32[]{:S(2)}) copy-start(s32[16]{0:T(128)} %copy-done.20) | copy-start | bytes 196
  240.1 27.7 %all-to-all-start.3 = ((bf16[16,51,1024]{2,1,0:T(8,128)(2,1)}), bf16[16,51,1024]{2,1,0:T(8,128)(2,1)}, u32[]{:S(2)}, u32[]{:S(2)}) async-start(bf16[16,51,1024]{2,1,0:T(8,128)(2,1)} %fusion.15), calls=%async_computation.3 | async-start | bytes 3670016 | tf_op jit(solution)/shard_map/all_to_all | solution.py:220
  267.8 3.3 %copy-start.9 = (bf16[640,1024]{1,0:T(8,128)(2,1)S(1)}, bf16[640,1024]{1,0:T(8,128)(2,1)}, u32[]{:S(2)}) copy-start(bf16[640,1024]{1,0:T(8,128)(2,1)} %bitcast_convert_fusion.1) | copy-start | bytes 3932164
  267.8 5.0 %copy-start.1 = (bf16[640,2048]{1,0:T(8,128)(2,1)S(1)}, bf16[640,2048]{1,0:T(8,128)(2,1)}, u32[]{:S(2)}) copy-start(bf16[640,2048]{1,0:T(8,128)(2,1)} %param.17) | copy-start | bytes 7864324
Sparse Core Ops, SparseCore 0:
  9.7 69.9 all-gather.1
